TPU v7x, 256 devices: a whole 4x4x8 slice. The times are simulated.
256 devices in a mesh: seq: 64 (over y, z, core), pb: 4 (over x).
Axes of the slice: x: 4, y: 4, z: 8, core: 2. Of those that a mesh axis runs over, the one named last changes fastest.
Arguments:
- tokens: bfloat16 [16384, 2048], P('seq'), may hold values from -0.119628906 to 0.119628906
- w_query: bfloat16 [2048, 2048], P(None, 'pb')
- w_key: bfloat16 [2048, 2048], P(None, 'pb')
- w_value: bfloat16 [2048, 2048], P(None, 'pb'), may hold values from -0.125 to 0.125
- w_out: bfloat16 [2048, 2048], P('pb'), may hold values from -0.125 to 0.125
- gain_attn: float32 [2048], replicated, may hold values from 0.1 to 1.9
- gain_embed: float32 [2048], replicated, may hold values from 0.1 to 1.9
- queries: bfloat16 [256, 32, 2048], P(('seq', 'pb')), may hold values from -0.125 to 0.125
- query_lengths: int32 [256], P(('seq', 'pb')), may hold values from 8 to 32
- group_lengths: int32 [128], replicated, may hold values from 1 to 1024, 16384 in all
- teacher: float32 [256, 128], P(('seq', 'pb')), may hold values from -12 to 12
Outputs:
- embedded: bfloat16 [16384, 2048], P('seq')
- scores: float32 [256, 128], P(('seq', 'pb'))
- score_gradient: float32 [256, 128], P(('seq', 'pb'))
- distill_loss: float32 [], replicated
Inputs may be any that keep to these rules, and one draw needn't show every extreme that they name: `group_lengths`: the groups cover the document in order: the lengths sum to 16384.
All inputs are finite; a program needn't handle non-finite values.
Results may differ from a plain program's by a relative error of at most 0.013.
Values may be sent and summed in bfloat16 or wider, within the bound.
No kernel may reach another device: no remote copies, remote signals or barrier semaphores. Data moves between devices by JAX's collectives and lax.ppermute only.
A program may use at most 128 MiB of HBM per device.

v0:
```python
import jax
import jax.numpy as jnp
from jax import lax
from jax.sharding import PartitionSpec as P

HD = 128
WIN = 2048
LQ = 32
EPSILON = 1e-06
SOFTMAX_TEMP = 0.1


def shifted_2(x, axis, by):
    count = lax.axis_size(axis)
    pairs = [(i, i + by) for i in range(count) if 0 <= i + by < count]
    return lax.ppermute(x, axis, pairs)


def rms_scale(values, gain):
    mean_sq = jnp.mean(values * values, axis=-1, keepdims=True)
    return values * lax.rsqrt(mean_sq + EPSILON) * gain


def segmented_max(values, group_id):
    span_len = values.shape[-1]
    stride = 1
    while stride < span_len:
        filler = jnp.full(values.shape[:-1] + (stride,), -jnp.inf, values.dtype)
        shifted = jnp.concatenate([filler, values[..., :-stride]], axis=-1)
        prior_id = jnp.concatenate([jnp.full((stride,), -1, jnp.int32), group_id[:-stride]])
        values = jnp.where((prior_id == group_id)[None, :], jnp.maximum(values, shifted), values)
        stride = stride * 2
    return values


def per_device(
    tokens,
    w_query,
    w_key,
    w_value,
    w_out,
    gain_attn,
    gain_embed,
    queries,
    query_lengths,
    group_lengths,
    teacher,
):
    shard_rows = tokens.shape[0]
    seq_count = lax.axis_size("seq")
    seq_place = lax.axis_index("seq")
    head_width = w_query.shape[1]
    heads_here = head_width // HD
    half_win = WIN // 2
    reach_count = half_win // shard_rows
    my_start = seq_place * shard_rows
    total_tokens = shard_rows * seq_count
    residual = tokens.astype(jnp.float32)
    normed = rms_scale(residual, gain_attn).astype(jnp.bfloat16)
    q_local = jnp.dot(normed, w_query, preferred_element_type=jnp.float32).astype(jnp.bfloat16)
    k_local = jnp.dot(normed, w_key, preferred_element_type=jnp.float32).astype(jnp.bfloat16)
    v_local = jnp.dot(normed, w_value, preferred_element_type=jnp.float32).astype(jnp.bfloat16)
    key_value = jnp.stack([k_local, v_local])
    earlier = [shifted_2(key_value, "seq", distance) for distance in range(reach_count, 0, -1)]
    later = [shifted_2(key_value, "seq", -distance) for distance in range(1, reach_count + 1)]
    window = jnp.concatenate(earlier + [key_value] + later, axis=1)
    span_rows = window.shape[1]
    q_pos = my_start + jnp.arange(shard_rows, dtype=jnp.int32)
    k_pos = my_start - reach_count * shard_rows + jnp.arange(span_rows, dtype=jnp.int32)
    in_window = (
        (jnp.abs(q_pos[:, None] - k_pos[None, :]) <= half_win)
        & (k_pos >= 0)[None, :]
        & (k_pos < total_tokens)[None, :]
    )
    q_heads = q_local.reshape(shard_rows, heads_here, HD)
    k_heads = window[0].reshape(span_rows, heads_here, HD)
    v_heads = window[1].reshape(span_rows, heads_here, HD)
    logits = jnp.einsum(
        "qhd,khd->hqk", q_heads, k_heads, preferred_element_type=jnp.float32
    ) * HD ** (-0.5)
    logits = jnp.where(in_window[None], logits, -jnp.inf)
    row_max = jnp.max(logits, axis=-1, keepdims=True)
    exp_terms = jnp.exp(logits - row_max)
    weights = (exp_terms / jnp.sum(exp_terms, axis=-1, keepdims=True)).astype(jnp.bfloat16)
    mixed = jnp.einsum("hqk,khd->qhd", weights, v_heads, preferred_element_type=jnp.float32)
    mixed = mixed.reshape(shard_rows, head_width).astype(jnp.bfloat16)
    partial_value = jnp.dot(mixed, w_out, preferred_element_type=jnp.float32)
    attn_sum = lax.psum(partial_value, "pb")
    embedded = rms_scale(residual + attn_sum, gain_embed).astype(jnp.bfloat16)
    group_end = jnp.cumsum(group_lengths)
    group_start = group_end - group_lengths
    group_id = jnp.sum((group_end[None, :] <= q_pos[:, None]).astype(jnp.int32), axis=1)
    last_local = jnp.clip(group_end - 1 - my_start, 0, shard_rows - 1)
    present = (group_start < my_start + shard_rows) & (group_end > my_start)
    q_piece = lax.all_gather(queries, "seq", axis=0, tiled=True)
    count = q_piece.shape[0]
    q_rows = q_piece.reshape(count * q_piece.shape[1], q_piece.shape[2])
    similar = jnp.einsum("td,rd->tr", q_rows, embedded, preferred_element_type=jnp.float32)
    running = segmented_max(similar, group_id)
    picked = jnp.take(running, last_local, axis=1)
    picked = jnp.where(present[None, :], picked, -jnp.inf)
    part_max = picked.reshape(count, q_piece.shape[1], picked.shape[-1])
    own_count = queries.shape[0]
    all_maxima = lax.pmax(part_max, "seq")
    token_max = lax.dynamic_slice_in_dim(all_maxima, seq_place * own_count, own_count, 0)
    live_mask = (jnp.arange(LQ, dtype=jnp.int32)[None, :] < query_lengths[:, None]).astype(
        jnp.float32
    )
    scores = (
        jnp.sum(token_max * live_mask[:, :, None], axis=1)
        / query_lengths.astype(jnp.float32)[:, None]
    )
    student_scores = scores / SOFTMAX_TEMP
    student_scores = student_scores - jnp.max(student_scores, axis=-1, keepdims=True)
    student_log_prob = student_scores - jnp.log(
        jnp.sum(jnp.exp(student_scores), axis=-1, keepdims=True)
    )
    target_scores = teacher / SOFTMAX_TEMP
    target_scores = target_scores - jnp.max(target_scores, axis=-1, keepdims=True)
    log_t = target_scores - jnp.log(jnp.sum(jnp.exp(target_scores), axis=-1, keepdims=True))
    teacher_prob = jnp.exp(log_t)
    kl_terms = jnp.sum(teacher_prob * (log_t - student_log_prob), axis=-1)
    query_count_all = own_count * seq_count * lax.axis_size("pb")
    distill_loss = lax.psum(jnp.sum(kl_terms), ("seq", "pb")) / query_count_all
    score_gradient = (jnp.exp(student_log_prob) - teacher_prob) / (SOFTMAX_TEMP * query_count_all)
    return (embedded, scores, score_gradient, distill_loss)


def solution(mesh):
    placed = (
        P("seq", None),
        P(None, "pb"),
        P(None, "pb"),
        P(None, "pb"),
        P("pb", None),
        P(),
        P(),
        P(("seq", "pb"), None, None),
        P(("seq", "pb")),
        P(),
        P(("seq", "pb"), None),
    )
    return jax.shard_map(
        per_device,
        mesh=mesh,
        in_specs=placed,
        out_specs=(P("seq", None), P(("seq", "pb"), None), P(("seq", "pb"), None), P()),
        check_vma=False,
    )
```

profile of v0, /device:TPU:1, one launch (start us, length us, event | category | flops | bytes accessed | tf_op | source)
XLA Modules:
  0.0 512.5 jit_solution(6274992664846566963)
XLA Ops:
  8.1 1.6 fusion.10
  9.8 2.8 fusion.15
  14.9 6.5 %collective-permute-start = (bf16[2,256,512]{2,1,0:T(8,128)(2,1)}, bf16[2,256,512]{2,1,0:T(8,128)(2,1)}, u32[]{:S(2)}, u32[]{:S(2)}) collective-permute-start(bf16[2,256,512]{2,1,0:T(8,128)(2,1)} %pad_maximum_fusion), channel_id=1, source_target_pairs={{0,16},{4,20},{8,24},{12,28},{16,32},{20,36},{24,40},{28,44},{32,4... | collective-permute-start | bytes 1572872 | tf_op jit(solution)/shard_map/ppermute | solution.py:16
  21.5 7.0 %collective-permute-start.1 = (bf16[2,256,512]{2,1,0:T(8,128)(2,1)}, bf16[2,256,512]{2,1,0:T(8,128)(2,1)}, u32[]{:S(2)}, u32[]{:S(2)}) collective-permute-start(bf16[2,256,512]{2,1,0:T(8,128)(2,1)} %pad_maximum_fusion), channel_id=1, source_target_pairs={{0,12},{4,16},{8,20},{12,24},{16,28},{20,32},{24,36},{28,40},{32,4... | collective-permute-start | bytes 1572872 | tf_op jit(solution)/shard_map/ppermute | solution.py:16
  28.4 2.6 collective-permute-start.2
  31.1 1.9 collective-permute-start.3
  33.0 3.2 collective-permute-start.4
  36.3 1.7 fusion.9
  37.9 3.0 fusion.16
  41.0 1.4 collective-permute-start.5
  43.5 14.3 %collective-permute-done.1 = bf16[2,256,512]{2,1,0:T(8,128)(2,1)} collective-permute-done((bf16[2,256,512]{2,1,0:T(8,128)(2,1)}, bf16[2,256,512]{2,1,0:T(8,128)(2,1)}, u32[]{:S(2)}, u32[]{:S(2)}) %collective-permute-start.1) | collective-permute-done | bytes 524320 | tf_op jit(solution)/shard_map/ppermute | solution.py:16
  57.7 1.3 collective-permute-start.6
  60.1 10.9 %collective-permute-done.2 = bf16[2,256,512]{2,1,0:T(8,128)(2,1)} collective-permute-done((bf16[2,256,512]{2,1,0:T(8,128)(2,1)}, bf16[2,256,512]{2,1,0:T(8,128)(2,1)}, u32[]{:S(2)}, u32[]{:S(2)}) %collective-permute-start.2) | collective-permute-done | bytes 524320 | tf_op jit(solution)/shard_map/ppermute | solution.py:16
  71.0 1.3 collective-permute-start.7
  73.3 4.4 collective-permute-done.3
  80.0 17.2 %collective-permute-done.6 = bf16[2,256,512]{2,1,0:T(8,128)(2,1)S(1)} collective-permute-done((bf16[2,256,512]{2,1,0:T(8,128)(2,1)}, bf16[2,256,512]{2,1,0:T(8,128)(2,1)S(1)}, u32[]{:S(2)}, u32[]{:S(2)}) %collective-permute-start.6) | collective-permute-done | bytes 524320 | tf_op jit(solution)/shard_map/ppermute | solution.py:16
  97.2 8.1 %collective-permute-done.7 = bf16[2,256,512]{2,1,0:T(8,128)(2,1)S(1)} collective-permute-done((bf16[2,256,512]{2,1,0:T(8,128)(2,1)}, bf16[2,256,512]{2,1,0:T(8,128)(2,1)S(1)}, u32[]{:S(2)}, u32[]{:S(2)}) %collective-permute-start.7) | collective-permute-done | bytes 524320 | tf_op jit(solution)/shard_map/ppermute | solution.py:16
  105.4 2.4 fusion.39
  107.8 4.3 copy.34
  112.1 5.3 %reshape_squeeze.7 = bf16[2304,4,128]{2,1,0:T(4,128)(2,1)} reshape(bf16[1,2304,512]{2,1,0:T(8,128)(2,1)} %get-tuple-element.8) | data formatting | bytes 4718592 | tf_op jit(solution)/shard_map/reshape;squeeze | solution.py:76
  117.4 8.8 %fusion.40 = (f32[4,256]{1,0:T(4,128)S(1)}, f32[4,256,2304]{2,1,0:T(8,128)}) fusion(pred[256,2304]{1,0:T(8,128)(4,1)} %fusion.9, bf16[2304,4,128]{2,1,0:T(4,128)(2,1)} %reshape_squeeze.7, bf16[32,4,8,128]{3,2,1,0:T(8,128)(2,1)S(1)} %copy-done.13), kind=kOutput, calls=%fused_computation.89 | convolution fusion | flops 613419264 | bytes 12652544 | tf_op jit(solution)/shard_map/sub | solution.py:83
  126.2 6.2 %fusion.13 = bf16[4,128,256]{2,1,0:T(8,128)(2,1)S(1)} fusion(bf16[2304,4,128]{0,2,1:T(8,128)(2,1)} %bitcast.54, f32[4,256,2304]{2,1,0:T(8,128)} %get-tuple-element.23, f32[4,256]{1,0:T(4,128)S(1)} %get-tuple-element.22), kind=kOutput, calls=%fused_computation.32 | convolution fusion | flops 608829440 | bytes 12062720 | tf_op jit(solution)/shard_map/hqk,khd->qhd/dot_general | solution.py:85
  132.4 2.0 fusion.45
  136.0 66.0 %all-reduce.18.cloned.1.call-done = f32[256,2048]{1,0:T(8,128)} async-done(((f32[256,2048]{1,0:T(8,128)}), f32[256,2048]{1,0:T(8,128)}) %all-reduce.18.cloned.1.call-update) | async-done | bytes 2097168 | tf_op jit(solution)/shard_map/psum | solution.py:88
  202.0 2.1 multiply_reduce_fusion
  204.7 20.3 %all-gather.2.cloned.1.call-done = bf16[64,32,2048]{2,1,0:T(8,128)(2,1)} async-done(((bf16[1,32,2048]{2,1,0:T(8,128)(2,1)}), bf16[64,32,2048]{2,1,0:T(8,128)(2,1)}) %all-gather.2.cloned.1.call-update) | async-done | bytes 8388624 | tf_op jit(solution)/shard_map/all_gather | solution.py:95
  225.0 5.7 %convolution_bitcast_fusion = f32[2048,256]{0,1:T(8,128)S(1)} fusion(bf16[256,2048]{1,0:T(8,128)(2,1)S(1)} %multiply_convert_fusion, bf16[2048,2048]{1,0:T(8,128)(2,1)} %bitcast.65), kind=kOutput, calls=%fused_computation.21 | convolution fusion | flops 2147483648 | bytes 11534336 | tf_op jit(solution)/shard_map/td,rd->tr/dot_general | solution.py:98
  235.2 1.4 copy.33
  236.6 2.4 select_select_fusion
  242.2 178.2 %all-reduce.20.cloned.1.call-done = f32[64,32,128]{2,1,0:T(8,128)} async-done(((f32[64,32,128]{2,1,0:T(8,128)}), f32[64,32,128]{2,1,0:T(8,128)}) %all-reduce.20.cloned.1.call-update) | async-done | bytes 1048592 | tf_op jit(solution)/shard_map/pmax | solution.py:104
  423.7 2.5 multiply_reduce_fusion.2
  426.2 77.1 %psum.15 = f32[]{:T(128)} all-reduce(f32[]{:T(128)} %get-tuple-element.10), channel_id=1, replica_groups=mesh['seq'=64,'pb'=4] {'seq','pb'}, use_global_device_ids=true, to_apply=%region_14.15 | all-reduce | flops 1 | bytes 8 | tf_op jit(solution)/shard_map/psum | solution.py:124
  (82 shorter events, 18.9 us)
Async XLA Ops:
  8.0 124.4 %copy-start = (bf16[512,2048]{1,0:T(8,128)(2,1)S(1)}, bf16[512,2048]{1,0:T(8,128)(2,1)}, u32[]{:S(2)}) copy-start(bf16[512,2048]{1,0:T(8,128)(2,1)} %param.15) | copy-start | bytes 6291460
  8.0 194.0 %all-reduce.18.cloned.1.call-start = ((), (), s32[]{:S(2)}) async-start(), calls=%async_computation | async-start | bytes 4194304 | tf_op jit(solution)/shard_map/psum | solution.py:88
  9.7 2.9 copy-start.2
  9.7 2.9 copy-start.11
  9.7 2.9 copy-start.12
  13.4 0.7 copy-start.5
  14.9 26.0 %collective-permute-start = (bf16[2,256,512]{2,1,0:T(8,128)(2,1)}, bf16[2,256,512]{2,1,0:T(8,128)(2,1)}, u32[]{:S(2)}, u32[]{:S(2)}) collective-permute-start(bf16[2,256,512]{2,1,0:T(8,128)(2,1)} %pad_maximum_fusion), channel_id=1, source_target_pairs={{0,16},{4,20},{8,24},{12,28},{16,32},{20,36},{24,40},{28,44},{32,4... | collective-permute-start | bytes 1572872 | tf_op jit(solution)/shard_map/ppermute | solution.py:16
  21.5 36.2 %collective-permute-start.1 = (bf16[2,256,512]{2,1,0:T(8,128)(2,1)}, bf16[2,256,512]{2,1,0:T(8,128)(2,1)}, u32[]{:S(2)}, u32[]{:S(2)}) collective-permute-start(bf16[2,256,512]{2,1,0:T(8,128)(2,1)} %pad_maximum_fusion), channel_id=1, source_target_pairs={{0,12},{4,16},{8,20},{12,24},{16,28},{20,32},{24,36},{28,40},{32,4... | collective-permute-start | bytes 1572872 | tf_op jit(solution)/shard_map/ppermute | solution.py:16
  28.4 42.5 %collective-permute-start.2 = (bf16[2,256,512]{2,1,0:T(8,128)(2,1)}, bf16[2,256,512]{2,1,0:T(8,128)(2,1)}, u32[]{:S(2)}, u32[]{:S(2)}) collective-permute-start(bf16[2,256,512]{2,1,0:T(8,128)(2,1)} %pad_maximum_fusion), channel_id=1, source_target_pairs={{0,8},{4,12},{8,16},{12,20},{16,24},{20,28},{24,32},{28,36},{32,40... | collective-permute-start | bytes 1572872 | tf_op jit(solution)/shard_map/ppermute | solution.py:16
  31.1 46.6 %collective-permute-start.3 = (bf16[2,256,512]{2,1,0:T(8,128)(2,1)}, bf16[2,256,512]{2,1,0:T(8,128)(2,1)}, u32[]{:S(2)}, u32[]{:S(2)}) collective-permute-start(bf16[2,256,512]{2,1,0:T(8,128)(2,1)} %pad_maximum_fusion), channel_id=1, source_target_pairs={{0,4},{4,8},{8,12},{12,16},{16,20},{20,24},{24,28},{28,32},{32,36}... | collective-permute-start | bytes 1572872 | tf_op jit(solution)/shard_map/ppermute | solution.py:16
  33.0 45.9 %collective-permute-start.4 = (bf16[2,256,512]{2,1,0:T(8,128)(2,1)}, bf16[2,256,512]{2,1,0:T(8,128)(2,1)}, u32[]{:S(2)}, u32[]{:S(2)}) collective-permute-start(bf16[2,256,512]{2,1,0:T(8,128)(2,1)} %pad_maximum_fusion), channel_id=1, source_target_pairs={{4,0},{8,4},{12,8},{16,12},{20,16},{24,20},{28,24},{32,28},{36,32}... | collective-permute-start | bytes 1572872 | tf_op jit(solution)/shard_map/ppermute | solution.py:16
  41.0 37.8 %copy-start.6 = (bf16[1,256,512]{2,1,0:T(8,128)(2,1)S(1)}, bf16[1,256,512]{2,1,0:T(8,128)(2,1)}, u32[]{:S(2)}) copy-start(bf16[1,256,512]{2,1,0:T(8,128)(2,1)} %copy-done.5) | copy-start | bytes 786436
  41.0 39.0 %collective-permute-start.5 = (bf16[2,256,512]{2,1,0:T(8,128)(2,1)}, bf16[2,256,512]{2,1,0:T(8,128)(2,1)S(1)}, u32[]{:S(2)}, u32[]{:S(2)}) collective-permute-start(bf16[2,256,512]{2,1,0:T(8,128)(2,1)} %pad_maximum_fusion), channel_id=1, source_target_pairs={{8,0},{12,4},{16,8},{20,12},{24,16},{28,20},{32,24},{36,28},{40,32... | collective-permute-start | bytes 1572872 | tf_op jit(solution)/shard_map/ppermute | solution.py:16
  57.7 39.4 %collective-permute-start.6 = (bf16[2,256,512]{2,1,0:T(8,128)(2,1)}, bf16[2,256,512]{2,1,0:T(8,128)(2,1)S(1)}, u32[]{:S(2)}, u32[]{:S(2)}) collective-permute-start(bf16[2,256,512]{2,1,0:T(8,128)(2,1)} %pad_maximum_fusion), channel_id=1, source_target_pairs={{12,0},{16,4},{20,8},{24,12},{28,16},{32,20},{36,24},{40,28},{44,3... | collective-permute-start | bytes 1572872 | tf_op jit(solution)/shard_map/ppermute | solution.py:16
  71.0 34.4 %collective-permute-start.7 = (bf16[2,256,512]{2,1,0:T(8,128)(2,1)}, bf16[2,256,512]{2,1,0:T(8,128)(2,1)S(1)}, u32[]{:S(2)}, u32[]{:S(2)}) collective-permute-start(bf16[2,256,512]{2,1,0:T(8,128)(2,1)} %pad_maximum_fusion), channel_id=1, source_target_pairs={{16,0},{20,4},{24,8},{28,12},{32,16},{36,20},{40,24},{44,28},{48,3... | collective-permute-start | bytes 1572872 | tf_op jit(solution)/shard_map/ppermute | solution.py:16
  112.1 5.3 %copy-start.13 = (bf16[32,4,8,128]{3,2,1,0:T(8,128)(2,1)S(1)}, bf16[32,4,8,128]{3,2,1,0:T(8,128)(2,1)}, u32[]{:S(2)}) copy-start(bf16[32,4,8,128]{3,2,1,0:T(8,128)(2,1)} %fusion.16) | copy-start | bytes 786436
  134.4 0.8 copy-start.8
  134.4 69.7 %copy-start.7 = (f32[2048]{0:T(1024)S(1)}, f32[2048]{0:T(1024)}, u32[]{:S(2)}) copy-start(f32[2048]{0:T(1024)} %param.17) | copy-start | bytes 24580
  134.5 90.5 %all-gather.2.cloned.1.call-start = ((), (), s32[]{:S(2)}) async-start(), calls=%async_computation.1 | async-start | bytes 8519680 | tf_op jit(solution)/shard_map/all_gather | solution.py:95
  135.0 285.3 %all-reduce.20.cloned.1.call-start = ((), (), s32[]{:S(2)}) async-start(), calls=%async_computation.2 | async-start | bytes 2097152 | tf_op jit(solution)/shard_map/pmax | solution.py:104
  202.0 2.3 copy-start.3
  204.6 26.1 %copy-start.4 = (bf16[256,2048]{1,0:T(8,128)(2,1)}, bf16[256,2048]{1,0:T(8,128)(2,1)S(1)}, u32[]{:S(2)}) copy-start(bf16[256,2048]{1,0:T(8,128)(2,1)S(1)} %multiply_convert_fusion) | copy-start | bytes 3145732
  235.2 268.7 %copy-start.1 = (bf16[512,2048]{1,0:T(8,128)(2,1)S(1)}, bf16[512,2048]{1,0:T(8,128)(2,1)}, u32[]{:S(2)}) copy-start(bf16[512,2048]{1,0:T(8,128)(2,1)} %param.15) | copy-start | bytes 6291460
  236.6 3.0 copy-start.10
  421.8 82.2 %copy-start.9 = (f32[128]{0:T(128)}, f32[128]{0:T(128)S(1)}, u32[]{:S(2)}) copy-start(f32[128]{0:T(128)S(1)} %get-tuple-element.7) | copy-start | bytes 1540
Sparse Core Ops, SparseCore 0:
  134.6 67.3 all-reduce.17
Sparse Core Ops, SparseCore 1:
  137.7 87.2 all-gather.1
  239.1 181.2 all-reduce.19
where the time goes:
time: 514 us; the launch traced here: 513 us
  waiting for transfers between devices  320 us (62%)
  blocking collectives  77.1 us (15%)
  matrix products  29.3 us (6%)
  starting transfers between devices  25.5 us (5%)
  local copies, waits for them, and re-layouts  21.7 us (4%)
  between operations  19.7 us (4%)
  other arithmetic  19.2 us (4%)
    pmax x1, waiting for transfers between devices, per_device(): all_maxima = lax.pmax(part_max, 'seq')  178 us
    psum x1, blocking collectives, per_device(): distill_loss = lax.psum(jnp.sum(kl_terms), ('seq', 'pb')) / query_count_all  77.1 us
    psum x1, waiting for transfers between devices, per_device(): attn_sum = lax.psum(partial_value, 'pb')  66 us
    ppermute x8, waiting for transfers between devices, shifted_2(): return lax.ppermute(x, axis, pairs)  54.8 us
    ppermute x8, starting transfers between devices, shifted_2(): return lax.ppermute(x, axis, pairs)  25.2 us
    all_gather x1, waiting for transfers between devices, per_device(): q_piece = lax.all_gather(queries, 'seq', axis=0, tiled=True)  20.3 us
  transfers between devices with their start and end apart: 11, of which 8 were waited for; matrix products, arithmetic and copies ran while one was open for 3% of the time, Pallas kernels for 0%

commit v1 on v0

--- a/solution.py
+++ b/solution.py
@@ -8,6 +8,15 @@
 LQ = 32
 EPSILON = 1e-06
 SOFTMAX_TEMP = 0.1
+
+
+def add_in_pairs(block, axis):
+    size = lax.axis_size(axis)
+    acc, reach = (block, 1)
+    while reach < size:
+        acc = acc + lax.ppermute(acc, axis, [(i, i ^ reach) for i in range(size)])
+        reach = 2 * reach
+    return acc
 
 
 def shifted_2(x, axis, by):
@@ -85,7 +94,7 @@
     mixed = jnp.einsum("hqk,khd->qhd", weights, v_heads, preferred_element_type=jnp.float32)
     mixed = mixed.reshape(shard_rows, head_width).astype(jnp.bfloat16)
     partial_value = jnp.dot(mixed, w_out, preferred_element_type=jnp.float32)
-    attn_sum = lax.psum(partial_value, "pb")
+    attn_sum = add_in_pairs(partial_value, "pb")
     embedded = rms_scale(residual + attn_sum, gain_embed).astype(jnp.bfloat16)
     group_end = jnp.cumsum(group_lengths)
     group_start = group_end - group_lengths

time: 514 us -> 555 us (1.080)
  waiting for transfers between devices: 320 us -> 357 us
    ppermute x0 -> x2, waiting for transfers between devices: none -> 86.8 us  [add_in_pairs(): acc = acc + lax.ppermute(acc, axis, [(i, i ^ reach) for i in range(size)])]
    psum x1 -> x0, waiting for transfers between devices: 66 us -> none  [per_device(): attn_sum = lax.psum(partial_value, 'pb')]
    ppermute x8, waiting for transfers between devices: 54.8 us -> 78.1 us  [shifted_2(): return lax.ppermute(x, axis, pairs)]
    all_gather x1, waiting for transfers between devices: 20.3 us -> 0.01 us  [per_device(): q_piece = lax.all_gather(queries, 'seq', axis=0, tiled=True)]
    pmax x1, waiting for transfers between devices: 178 us -> 191 us  [per_device(): all_maxima = lax.pmax(part_max, 'seq')]
  transfers between devices with their start and end apart: 11 -> 12, of which waited for: 8 -> 8; matrix products, arithmetic and copies ran while one was open for 3% -> 9% of each run, Pallas kernels for 0% -> 0%
where the time goes in v1:
time: 555 us; the launch traced here: 554 us
  waiting for transfers between devices  357 us (64%)
  blocking collectives  77.2 us (14%)
  starting transfers between devices  29.4 us (5%)
  matrix products  28.4 us (5%)
  other arithmetic  22 us (4%)
  local copies, waits for them, and re-layouts  21.7 us (4%)
  between operations  18.3 us (3%)
    pmax x1, waiting for transfers between devices, per_device(): all_maxima = lax.pmax(part_max, 'seq')  191 us
    ppermute x2, waiting for transfers between devices, add_in_pairs(): acc = acc + lax.ppermute(acc, axis, [(i, i ^ reach) for i in range(size)])  86.8 us
    ppermute x8, waiting for transfers between devices, shifted_2(): return lax.ppermute(x, axis, pairs)  78.1 us
    psum x1, blocking collectives, per_device(): distill_loss = lax.psum(jnp.sum(kl_terms), ('seq', 'pb')) / query_count_all  77.2 us
    ppermute x8, starting transfers between devices, shifted_2(): return lax.ppermute(x, axis, pairs)  25.2 us
  transfers between devices with their start and end apart: 12, of which 8 were waited for; matrix products, arithmetic and copies ran while one was open for 9% of the time, Pallas kernels for 0%

profile of v1, /device:TPU:1, one launch (start us, length us, event | category | flops | bytes accessed | tf_op | source)
XLA Modules:
  0.0 553.5 jit_solution(8464645964514912757)
XLA Ops:
  8.0 1.5 fusion.10
  9.5 2.8 fusion.15
  14.7 6.5 %collective-permute-start = (bf16[2,256,512]{2,1,0:T(8,128)(2,1)}, bf16[2,256,512]{2,1,0:T(8,128)(2,1)}, u32[]{:S(2)}, u32[]{:S(2)}) collective-permute-start(bf16[2,256,512]{2,1,0:T(8,128)(2,1)} %pad_maximum_fusion), channel_id=1, source_target_pairs={{0,16},{4,20},{8,24},{12,28},{16,32},{20,36},{24,40},{28,44},{32,4... | collective-permute-start | bytes 1572872 | tf_op jit(solution)/shard_map/ppermute | solution.py:25
  21.2 7.0 %collective-permute-start.1 = (bf16[2,256,512]{2,1,0:T(8,128)(2,1)}, bf16[2,256,512]{2,1,0:T(8,128)(2,1)}, u32[]{:S(2)}, u32[]{:S(2)}) collective-permute-start(bf16[2,256,512]{2,1,0:T(8,128)(2,1)} %pad_maximum_fusion), channel_id=1, source_target_pairs={{0,12},{4,16},{8,20},{12,24},{16,28},{20,32},{24,36},{28,40},{32,4... | collective-permute-start | bytes 1572872 | tf_op jit(solution)/shard_map/ppermute | solution.py:25
  28.2 2.6 collective-permute-start.2
  30.8 1.9 collective-permute-start.3
  32.7 3.2 collective-permute-start.4
  36.0 1.7 fusion.9
  37.7 3.1 fusion.16
  40.7 1.4 collective-permute-start.5
  43.2 19.2 %collective-permute-done.1 = bf16[2,256,512]{2,1,0:T(8,128)(2,1)} collective-permute-done((bf16[2,256,512]{2,1,0:T(8,128)(2,1)}, bf16[2,256,512]{2,1,0:T(8,128)(2,1)}, u32[]{:S(2)}, u32[]{:S(2)}) %collective-permute-start.1) | collective-permute-done | bytes 524320 | tf_op jit(solution)/shard_map/ppermute | solution.py:25
  62.4 1.3 collective-permute-start.6
  64.8 13.6 %collective-permute-done.2 = bf16[2,256,512]{2,1,0:T(8,128)(2,1)} collective-permute-done((bf16[2,256,512]{2,1,0:T(8,128)(2,1)}, bf16[2,256,512]{2,1,0:T(8,128)(2,1)}, u32[]{:S(2)}, u32[]{:S(2)}) %collective-permute-start.2) | collective-permute-done | bytes 524320 | tf_op jit(solution)/shard_map/ppermute | solution.py:25
  80.7 10.8 %collective-permute-done.3 = bf16[2,256,512]{2,1,0:T(8,128)(2,1)} collective-permute-done((bf16[2,256,512]{2,1,0:T(8,128)(2,1)}, bf16[2,256,512]{2,1,0:T(8,128)(2,1)}, u32[]{:S(2)}, u32[]{:S(2)}) %collective-permute-start.3) | collective-permute-done | bytes 524320 | tf_op jit(solution)/shard_map/ppermute | solution.py:25
  93.8 9.0 %collective-permute-done.6 = bf16[2,256,512]{2,1,0:T(8,128)(2,1)S(1)} collective-permute-done((bf16[2,256,512]{2,1,0:T(8,128)(2,1)}, bf16[2,256,512]{2,1,0:T(8,128)(2,1)S(1)}, u32[]{:S(2)}, u32[]{:S(2)}) %collective-permute-start.6) | collective-permute-done | bytes 524320 | tf_op jit(solution)/shard_map/ppermute | solution.py:25
  102.8 25.6 %collective-permute-done.7 = bf16[2,256,512]{2,1,0:T(8,128)(2,1)S(1)} collective-permute-done((bf16[2,256,512]{2,1,0:T(8,128)(2,1)}, bf16[2,256,512]{2,1,0:T(8,128)(2,1)S(1)}, u32[]{:S(2)}, u32[]{:S(2)}) %collective-permute-start.7) | collective-permute-done | bytes 524320 | tf_op jit(solution)/shard_map/ppermute | solution.py:25
  128.4 2.4 fusion.39
  130.9 4.4 copy.34
  135.2 5.3 reshape_squeeze.7
  140.6 8.8 %fusion.40 = (f32[4,256]{1,0:T(4,128)S(1)}, f32[4,256,2304]{2,1,0:T(8,128)}) fusion(pred[256,2304]{1,0:T(8,128)(4,1)} %fusion.9, bf16[2304,4,128]{2,1,0:T(4,128)(2,1)} %reshape_squeeze.7, bf16[32,4,8,128]{3,2,1,0:T(8,128)(2,1)S(1)} %copy-done.11), kind=kOutput, calls=%fused_computation.89 | convolution fusion | flops 613419264 | bytes 12652544 | tf_op jit(solution)/shard_map/sub | solution.py:92
  149.4 6.1 %fusion.13 = bf16[4,128,256]{2,1,0:T(8,128)(2,1)S(1)} fusion(bf16[2304,4,128]{0,2,1:T(8,128)(2,1)} %bitcast.54, f32[4,256,2304]{2,1,0:T(8,128)} %get-tuple-element.23, f32[4,256]{1,0:T(4,128)S(1)} %get-tuple-element.22), kind=kOutput, calls=%fused_computation.32 | convolution fusion | flops 608829440 | bytes 12062720 | tf_op jit(solution)/shard_map/hqk,khd->qhd/dot_general | solution.py:94
  157.5 42.7 %collective-permute-done.8 = f32[256,2048]{1,0:T(8,128)S(1)} collective-permute-done((f32[256,2048]{1,0:T(8,128)S(1)}, f32[256,2048]{1,0:T(8,128)S(1)}, u32[]{:S(2)}, u32[]{:S(2)}) %collective-permute-start.8) | collective-permute-done | bytes 2097184 | tf_op jit(solution)/shard_map/ppermute | solution.py:17
  200.5 2.9 collective-permute-start.9
  204.1 44.1 %collective-permute-done.9 = f32[256,2048]{1,0:T(8,128)} collective-permute-done((f32[256,2048]{1,0:T(8,128)S(1)}, f32[256,2048]{1,0:T(8,128)}, u32[]{:S(2)}, u32[]{:S(2)}) %collective-permute-start.9) | collective-permute-done | bytes 2097184 | tf_op jit(solution)/shard_map/ppermute | solution.py:17
  248.2 2.0 multiply_reduce_fusion
  250.2 3.1 multiply_convert_fusion
  253.3 6.1 %convolution_bitcast_fusion = f32[2048,256]{0,1:T(8,128)S(1)} fusion(bf16[256,2048]{1,0:T(8,128)(2,1)} %multiply_convert_fusion, bf16[2048,2048]{1,0:T(8,128)(2,1)} %bitcast.65), kind=kOutput, calls=%fused_computation.21 | convolution fusion | flops 2147483648 | bytes 11534336 | tf_op jit(solution)/shard_map/td,rd->tr/dot_general | solution.py:107
  263.9 1.4 copy.33
  265.3 2.4 select_select_fusion
  270.9 191.0 %all-reduce.17.cloned.1.call-done = f32[64,32,128]{2,1,0:T(8,128)} async-done(((f32[64,32,128]{2,1,0:T(8,128)}), f32[64,32,128]{2,1,0:T(8,128)}) %all-reduce.17.cloned.1.call-update) | async-done | bytes 1048592 | tf_op jit(solution)/shard_map/pmax | solution.py:113
  465.2 2.5 multiply_reduce_fusion.2
  467.7 77.2 %psum.7 = f32[]{:T(128)} all-reduce(f32[]{:T(128)} %get-tuple-element.10), channel_id=1, replica_groups=mesh['seq'=64,'pb'=4] {'seq','pb'}, use_global_device_ids=true, to_apply=%region_13.14 | all-reduce | flops 1 | bytes 8 | tf_op jit(solution)/shard_map/psum | solution.py:133
  (80 shorter events, 21.8 us)
Async XLA Ops:
  7.2 148.4 %copy-start = (bf16[512,2048]{1,0:T(8,128)(2,1)S(1)}, bf16[512,2048]{1,0:T(8,128)(2,1)}, u32[]{:S(2)}) copy-start(bf16[512,2048]{1,0:T(8,128)(2,1)} %param.15) | copy-start | bytes 6291460
  7.2 246.1 %all-gather.2.cloned.1.call-start = ((), (), s32[]{:S(2)}) async-start(), calls=%async_computation | async-start | bytes 8519680 | tf_op jit(solution)/shard_map/all_gather | solution.py:104
  7.9 454.0 %all-reduce.17.cloned.1.call-start = ((), (), s32[]{:S(2)}) async-start(), calls=%async_computation.1 | async-start | bytes 2097152 | tf_op jit(solution)/shard_map/pmax | solution.py:113
  9.5 2.9 copy-start.2
  9.5 2.9 copy-start.9
  9.5 2.9 copy-start.10
  13.1 0.7 copy-start.3
  14.7 26.0 %collective-permute-start = (bf16[2,256,512]{2,1,0:T(8,128)(2,1)}, bf16[2,256,512]{2,1,0:T(8,128)(2,1)}, u32[]{:S(2)}, u32[]{:S(2)}) collective-permute-start(bf16[2,256,512]{2,1,0:T(8,128)(2,1)} %pad_maximum_fusion), channel_id=1, source_target_pairs={{0,16},{4,20},{8,24},{12,28},{16,32},{20,36},{24,40},{28,44},{32,4... | collective-permute-start | bytes 1572872 | tf_op jit(solution)/shard_map/ppermute | solution.py:25
  21.2 41.2 %collective-permute-start.1 = (bf16[2,256,512]{2,1,0:T(8,128)(2,1)}, bf16[2,256,512]{2,1,0:T(8,128)(2,1)}, u32[]{:S(2)}, u32[]{:S(2)}) collective-permute-start(bf16[2,256,512]{2,1,0:T(8,128)(2,1)} %pad_maximum_fusion), channel_id=1, source_target_pairs={{0,12},{4,16},{8,20},{12,24},{16,28},{20,32},{24,36},{28,40},{32,4... | collective-permute-start | bytes 1572872 | tf_op jit(solution)/shard_map/ppermute | solution.py:25
  28.2 50.2 %collective-permute-start.2 = (bf16[2,256,512]{2,1,0:T(8,128)(2,1)}, bf16[2,256,512]{2,1,0:T(8,128)(2,1)}, u32[]{:S(2)}, u32[]{:S(2)}) collective-permute-start(bf16[2,256,512]{2,1,0:T(8,128)(2,1)} %pad_maximum_fusion), channel_id=1, source_target_pairs={{0,8},{4,12},{8,16},{12,20},{16,24},{20,28},{24,32},{28,36},{32,40... | collective-permute-start | bytes 1572872 | tf_op jit(solution)/shard_map/ppermute | solution.py:25
  30.8 60.7 %collective-permute-start.3 = (bf16[2,256,512]{2,1,0:T(8,128)(2,1)}, bf16[2,256,512]{2,1,0:T(8,128)(2,1)}, u32[]{:S(2)}, u32[]{:S(2)}) collective-permute-start(bf16[2,256,512]{2,1,0:T(8,128)(2,1)} %pad_maximum_fusion), channel_id=1, source_target_pairs={{0,4},{4,8},{8,12},{12,16},{16,20},{20,24},{24,28},{28,32},{32,36}... | collective-permute-start | bytes 1572872 | tf_op jit(solution)/shard_map/ppermute | solution.py:25
  32.7 60.0 %collective-permute-start.4 = (bf16[2,256,512]{2,1,0:T(8,128)(2,1)}, bf16[2,256,512]{2,1,0:T(8,128)(2,1)}, u32[]{:S(2)}, u32[]{:S(2)}) collective-permute-start(bf16[2,256,512]{2,1,0:T(8,128)(2,1)} %pad_maximum_fusion), channel_id=1, source_target_pairs={{4,0},{8,4},{12,8},{16,12},{20,16},{24,20},{28,24},{32,28},{36,32}... | collective-permute-start | bytes 1572872 | tf_op jit(solution)/shard_map/ppermute | solution.py:25
  40.7 51.9 %copy-start.4 = (bf16[1,256,512]{2,1,0:T(8,128)(2,1)S(1)}, bf16[1,256,512]{2,1,0:T(8,128)(2,1)}, u32[]{:S(2)}) copy-start(bf16[1,256,512]{2,1,0:T(8,128)(2,1)} %copy-done.3) | copy-start | bytes 786436
  40.7 53.1 %collective-permute-start.5 = (bf16[2,256,512]{2,1,0:T(8,128)(2,1)}, bf16[2,256,512]{2,1,0:T(8,128)(2,1)S(1)}, u32[]{:S(2)}, u32[]{:S(2)}) collective-permute-start(bf16[2,256,512]{2,1,0:T(8,128)(2,1)} %pad_maximum_fusion), channel_id=1, source_target_pairs={{8,0},{12,4},{16,8},{20,12},{24,16},{28,20},{32,24},{36,28},{40,32... | collective-permute-start | bytes 1572872 | tf_op jit(solution)/shard_map/ppermute | solution.py:25
  62.4 40.4 %collective-permute-start.6 = (bf16[2,256,512]{2,1,0:T(8,128)(2,1)}, bf16[2,256,512]{2,1,0:T(8,128)(2,1)S(1)}, u32[]{:S(2)}, u32[]{:S(2)}) collective-permute-start(bf16[2,256,512]{2,1,0:T(8,128)(2,1)} %pad_maximum_fusion), channel_id=1, source_target_pairs={{12,0},{16,4},{20,8},{24,12},{28,16},{32,20},{36,24},{40,28},{44,3... | collective-permute-start | bytes 1572872 | tf_op jit(solution)/shard_map/ppermute | solution.py:25
  78.3 50.1 %collective-permute-start.7 = (bf16[2,256,512]{2,1,0:T(8,128)(2,1)}, bf16[2,256,512]{2,1,0:T(8,128)(2,1)S(1)}, u32[]{:S(2)}, u32[]{:S(2)}) collective-permute-start(bf16[2,256,512]{2,1,0:T(8,128)(2,1)} %pad_maximum_fusion), channel_id=1, source_target_pairs={{16,0},{20,4},{24,8},{28,12},{32,16},{36,20},{40,24},{44,28},{48,3... | collective-permute-start | bytes 1572872 | tf_op jit(solution)/shard_map/ppermute | solution.py:25
  135.2 5.3 copy-start.11
  156.3 47.1 %copy-start.6 = (s32[128]{0:T(128)S(1)}, s32[128]{0:T(128)}, u32[]{:S(2)}) copy-start(s32[128]{0:T(128)} %param.20) | copy-start | bytes 1540
  156.3 43.9 %collective-permute-start.8 = (f32[256,2048]{1,0:T(8,128)S(1)}, f32[256,2048]{1,0:T(8,128)S(1)}, u32[]{:S(2)}, u32[]{:S(2)}) collective-permute-start(f32[256,2048]{1,0:T(8,128)S(1)} %fusion.45), channel_id=1, source_target_pairs={{0,1},{1,0},{2,3},{3,2},{4,5},{5,4},{6,7},{7,6},{8,9},{9,8},{10,11... | collective-permute-start | bytes 6291464 | tf_op jit(solution)/shard_map/ppermute | solution.py:17
  200.5 47.7 %collective-permute-start.9 = (f32[256,2048]{1,0:T(8,128)S(1)}, f32[256,2048]{1,0:T(8,128)}, u32[]{:S(2)}, u32[]{:S(2)}) collective-permute-start(f32[256,2048]{1,0:T(8,128)S(1)} %add.126), channel_id=1, source_target_pairs={{0,2},{1,3},{2,0},{3,1},{4,6},{5,7},{6,4},{7,5},{8,10},{9,11},{10,... | collective-permute-start | bytes 6291464 | tf_op jit(solution)/shard_map/ppermute | solution.py:17
  204.1 46.1 %copy-start.5 = (f32[2048]{0:T(1024)S(1)}, f32[2048]{0:T(1024)}, u32[]{:S(2)}) copy-start(f32[2048]{0:T(1024)} %param.17) | copy-start | bytes 24580
  263.9 281.7 %copy-start.1 = (bf16[512,2048]{1,0:T(8,128)(2,1)S(1)}, bf16[512,2048]{1,0:T(8,128)(2,1)}, u32[]{:S(2)}) copy-start(bf16[512,2048]{1,0:T(8,128)(2,1)} %param.15) | copy-start | bytes 6291460
  265.3 3.0 copy-start.8
  463.3 82.3 %copy-start.7 = (f32[128]{0:T(128)}, f32[128]{0:T(128)S(1)}, u32[]{:S(2)}) copy-start(f32[128]{0:T(128)S(1)} %get-tuple-element.7) | copy-start | bytes 1540
Sparse Core Ops, SparseCore 0:
  10.8 119.5 all-gather.1
  267.8 194.0 all-reduce.16
